TPU v7x, 256 devices: a whole 4x4x8 slice. The times are simulated.
256 devices in a mesh: dp: 16 (over z_lo, x), tensor: 16 (over y, z_hi, core).
Axes of the slice: x: 4, y: 4, z: 8 (z_hi: 2, z_lo: 4; z = z_hi * 4 + z_lo), core: 2. Of those that a mesh axis runs over, the one named last changes fastest.
Arguments:
- inner_x: bfloat16 [16, 2048, 7168], P('dp', None, 'tensor')
- gate_z: bfloat16 [16, 2048, 7168], P('dp', None, 'tensor'), may hold values from -6 to 6
- input_b: bfloat16 [16, 2048, 128], P('dp'), may hold values from -0.75 to 0.75
- output_c: bfloat16 [16, 2048, 128], P('dp'), may hold values from -6 to 6
- step_raw: float32 [16, 2048, 112], P('dp', None, 'tensor'), may hold values from -6 to 6
- decay_rate: float32 [112], P('tensor'), may hold values from 0.001 to 0.05
- skip_gain: float32 [112], P('tensor'), may hold values from 0.5 to 1.5
- norm_gain: float32 [7168], P('tensor'), may hold values from 0.5 to 1.5
- out_weight: bfloat16 [7168, 3584], P('tensor'), may hold values from -0.0625 to 0.0625
- segment: int32 [16, 2048], P('dp'), may hold values from 0 to 7, never falling along the last dimension, each value on 1 to 1024 neighbouring positions
- cache_slot: int32 [16, 8], replicated, may hold values from 0 to 127, as said below
Outputs:
- mixed: bfloat16 [16, 2048, 3584], P('dp', 'tensor')
- cache: float32 [128, 112, 4096], P('dp', 'tensor')
Inputs may be any that keep to these rules, and one draw needn't show every extreme that they name: `segment`: in each group's row the prompt numbers never fall and every prompt 0 to 7 is present. `cache_slot`: every slot is named exactly once; slot // 8 is the owning group, and no two prompts of one group have the same owning group.
All inputs are finite; a program needn't handle non-finite values.
Results may differ from a plain program's by a relative error of at most 0.018.
Values may be sent and summed in bfloat16 or wider, within the bound.
No kernel may reach another device: no remote copies, remote signals or barrier semaphores. Data moves between devices by JAX's collectives and lax.ppermute only.
A program may use at most 192 MiB of HBM per device.

v0:
```python
import jax
import jax.numpy as jnp
from jax import lax
from jax.sharding import PartitionSpec as P

HEADS = 112
HEAD = 64
STATE = 64
NGROUPS = 2
REQS = 8
BLOCK = 256
INNER = 7168
HIGHEST = lax.Precision.HIGHEST


def split_pair(values):
    upper = values.astype(jnp.bfloat16)
    lower = (values - upper.astype(jnp.float32)).astype(jnp.bfloat16)
    return (upper, lower)


def split_einsum(form, wide, narrow):
    upper, lower = split_pair(wide)
    first = jnp.einsum(form, upper, narrow, preferred_element_type=jnp.float32)
    return first + jnp.einsum(form, lower, narrow, preferred_element_type=jnp.float32)


def local(
    inner_x,
    gate_z,
    input_b,
    output_c,
    step_raw,
    decay_rate,
    skip_gain,
    norm_gain,
    out_weight,
    segment,
    cache_slot,
):
    stream_len = inner_x.shape[1]
    dev_width = inner_x.shape[2]
    dev_heads = decay_rate.shape[0]
    tensor_idx = lax.axis_index("tensor")
    group_idx = tensor_idx * dev_heads // (HEADS // NGROUPS)
    b_cols = lax.dynamic_slice_in_dim(input_b[0], group_idx * STATE, STATE, 1)
    c_cols = lax.dynamic_slice_in_dim(output_c[0], group_idx * STATE, STATE, 1)
    step_size = jax.nn.softplus(step_raw[0])
    cum_log = jnp.cumsum(-decay_rate[None, :] * step_size, axis=0)
    seg_row = segment[0]
    block_count = stream_len // BLOCK
    prev_cum = jnp.concatenate([jnp.zeros((1, dev_heads), jnp.float32), cum_log[:-1]], axis=0)[
        ::BLOCK
    ]
    prev_seg = jnp.concatenate([jnp.full((1,), -1, seg_row.dtype), seg_row[:-1]], axis=0)[::BLOCK]
    block_inputs = (
        inner_x[0].reshape(block_count, BLOCK, dev_heads, HEAD),
        cum_log.reshape(block_count, BLOCK, dev_heads),
        step_size.reshape(block_count, BLOCK, dev_heads),
        seg_row.reshape(block_count, BLOCK),
        b_cols.reshape(block_count, BLOCK, STATE),
        c_cols.reshape(block_count, BLOCK, STATE),
        prev_cum,
        prev_seg,
    )
    positions = jnp.arange(BLOCK)

    def advance(carried, block_in):
        x_blk, cum_blk, step_blk, seg_blk, b_blk, c_blk, prev_c, prev_s = block_in
        scores = jnp.dot(c_blk, b_blk.T, preferred_element_type=jnp.float32)
        causal_mask = (positions[None, :] <= positions[:, None]) & (
            seg_blk[:, None] == seg_blk[None, :]
        )
        log_gap = cum_blk.T[:, :, None] - cum_blk.T[:, None, :]
        weights = (
            jnp.exp(jnp.where(causal_mask[None], log_gap, -jnp.inf))
            * step_blk.T[:, None, :]
            * scores[None]
        )
        intra_part = split_einsum("hts,shp->thp", weights, x_blk)
        live_rows = (seg_blk == prev_s).astype(jnp.float32)
        carry_decay = jnp.exp(cum_blk - prev_c[None, :]) * live_rows[:, None]
        carry_part = split_einsum("hpn,tn->thp", carried, c_blk) * carry_decay[:, :, None]
        outputs = intra_part + carry_part + skip_gain[None, :, None] * x_blk.astype(jnp.float32)
        last_seg = seg_blk[-1]
        last_cum = cum_blk[-1]
        keep_rows = (last_seg == prev_s).astype(jnp.float32)
        pull_back = (
            jnp.exp(last_cum[None, :] - cum_blk)
            * step_blk
            * (seg_blk == last_seg).astype(jnp.float32)[:, None]
        )
        added_part = split_einsum("shp,sn->hpn", pull_back[:, :, None] * x_blk, b_blk)
        carried = carried * (jnp.exp(last_cum - prev_c) * keep_rows)[:, None, None] + added_part
        return (carried, outputs)

    _, outputs = lax.scan(advance, jnp.zeros((dev_heads, HEAD, STATE), jnp.float32), block_inputs)
    mixer_y = outputs.reshape(stream_len, dev_width)
    members = (seg_row[None, :] == jnp.arange(REQS)[:, None]).astype(jnp.float32)
    end_index = (
        jnp.sum((seg_row[None, :] <= jnp.arange(REQS)[:, None]).astype(jnp.int32), axis=1) - 1
    )
    at_end = (jnp.arange(stream_len)[None, :] == end_index[:, None]).astype(jnp.float32)
    end_cum = jnp.dot(at_end, cum_log, precision=HIGHEST)
    seg_end_cum = jnp.dot(members.T, end_cum, precision=HIGHEST)
    pull_all = jnp.exp(seg_end_cum - cum_log) * step_size
    weighted = (inner_x[0].reshape(stream_len, dev_heads, HEAD) * pull_all[:, :, None]).reshape(
        stream_len, dev_width
    )
    masked_b = (
        (members.astype(jnp.bfloat16)[:, :, None] * b_cols[None])
        .transpose(1, 0, 2)
        .reshape(stream_len, REQS * STATE)
    )
    finals = split_einsum("tc,tk->ck", weighted, masked_b)
    finals = (
        finals.reshape(dev_heads, HEAD, REQS, STATE)
        .transpose(2, 0, 1, 3)
        .reshape(REQS, dev_heads * HEAD * STATE)
    )
    gated = mixer_y * jax.nn.silu(gate_z[0].astype(jnp.float32))
    sum_sq = jnp.sum(gated * gated, axis=1)
    group_hot = (jnp.arange(NGROUPS) == group_idx).astype(jnp.float32)
    group_stat = lax.psum(sum_sq[:, None] * group_hot[None, :], "tensor")
    mean_sq = jnp.sum(group_stat * group_hot[None, :], axis=1) / (INNER // NGROUPS)
    rounded = (gated * lax.rsqrt(mean_sq + 1e-05)[:, None] * norm_gain[None, :]).astype(
        jnp.bfloat16
    )
    projected = lax.psum_scatter(
        jnp.dot(rounded, out_weight, preferred_element_type=jnp.float32).astype(jnp.bfloat16),
        "tensor",
        scatter_dimension=0,
        tiled=True,
    )
    mixed = projected[None]
    dp_idx = lax.axis_index("dp")
    dp_size = lax.axis_size("dp")
    own_slots = lax.dynamic_slice_in_dim(cache_slot, dp_idx, 1, 0)[0]
    dest_hot = ((own_slots // REQS)[:, None] == jnp.arange(dp_size)[None, :]).astype(jnp.float32)
    outbound = jnp.dot(dest_hot.T, finals, precision=HIGHEST).reshape(
        dp_size, dev_heads, HEAD * STATE
    )
    inbound = lax.all_to_all(
        outbound.astype(jnp.bfloat16), "dp", split_axis=0, concat_axis=0, tiled=True
    ).astype(outbound.dtype)
    wanted = dp_idx * REQS + jnp.arange(REQS)
    take_hot = jnp.any(cache_slot[:, :, None] == wanted[None, None, :], axis=1).astype(jnp.float32)
    cache = jnp.dot(
        take_hot.T, inbound.reshape(dp_size, dev_heads * HEAD * STATE), precision=HIGHEST
    )
    return (mixed, cache.reshape(REQS, dev_heads, HEAD * STATE))


def solution(mesh):
    in_specs = (
        P("dp", None, "tensor"),
        P("dp", None, "tensor"),
        P("dp", None, None),
        P("dp", None, None),
        P("dp", None, "tensor"),
        P("tensor"),
        P("tensor"),
        P("tensor"),
        P("tensor", None),
        P("dp", None),
        P(),
    )
    out_specs = (P("dp", "tensor", None), P("dp", "tensor", None))
    return jax.shard_map(local, mesh=mesh, in_specs=in_specs, out_specs=out_specs, check_vma=False)
```

profile of v0, /device:TPU:32, one launch (start us, length us, event | category | flops | bytes accessed | tf_op | source)
XLA Modules:
  0.0 556.6 jit_solution(15308856619682689794)
XLA Ops:
  7.8 2.8 constant_dynamic-slice_fusion.3
  16.4 2.0 reduce-window.6
  21.2 2.1 copy.87
  30.0 217.2 %while.13 = (s32[]{:T(128)}, f32[7,64,64]{2,1,0:T(8,128)S(1)}, f32[8,256,7,64]{1,0,3,2:T(8,128)}, f32[8,256,7]{1,2,0:T(8,128)S(1)}, f32[8,7]{1,0:T(8,128)S(1)}, ...) while((s32[]{:T(128)}, f32[7,64,64]{2,1,0:T(8,128)S(1)}, ...), condition=%wide.region_3.4_spmd.clone, body=%wide.region_2.3_spmd.clone.sunk | while | flops 192841488 | bytes 8220087 | solution.py:97
  43.5 11.3 %dynamic_update_slice.6 = f32[8,256,7,64]{1,0,3,2:T(8,128)} dynamic-update-slice(f32[8,256,7,64]{1,0,3,2:T(8,128)} %get-tuple-element.315, f32[1,256,7,64]{1,0,3,2:T(1,128)} %copy.140, s32[]{:T(128)} %get-tuple-element.313, s32[]{:T(128)} %constant.69.clone.1..sunk, s32[]{:T(128)} %constant.69.clone.1..sunk, s32[]{:T(128)} %constant.69.clone.1..sunk) | dynamic-update-slice | bytes 917508 | tf_op jit(solution)/shard_map/while/body/jit(dynamic_update_index_in_dim)/dynamic_update_slice | solution.py:97
  70.7 11.3 %dynamic_update_slice.6 = f32[8,256,7,64]{1,0,3,2:T(8,128)} dynamic-update-slice(f32[8,256,7,64]{1,0,3,2:T(8,128)} %get-tuple-element.315, f32[1,256,7,64]{1,0,3,2:T(1,128)} %copy.140, s32[]{:T(128)} %get-tuple-element.313, s32[]{:T(128)} %constant.69.clone.1..sunk, s32[]{:T(128)} %constant.69.clone.1..sunk, s32[]{:T(128)} %constant.69.clone.1..sunk) | dynamic-update-slice | bytes 917508 | tf_op jit(solution)/shard_map/while/body/jit(dynamic_update_index_in_dim)/dynamic_update_slice | solution.py:97
  97.8 11.3 %dynamic_update_slice.6 = f32[8,256,7,64]{1,0,3,2:T(8,128)} dynamic-update-slice(f32[8,256,7,64]{1,0,3,2:T(8,128)} %get-tuple-element.315, f32[1,256,7,64]{1,0,3,2:T(1,128)} %copy.140, s32[]{:T(128)} %get-tuple-element.313, s32[]{:T(128)} %constant.69.clone.1..sunk, s32[]{:T(128)} %constant.69.clone.1..sunk, s32[]{:T(128)} %constant.69.clone.1..sunk) | dynamic-update-slice | bytes 917508 | tf_op jit(solution)/shard_map/while/body/jit(dynamic_update_index_in_dim)/dynamic_update_slice | solution.py:97
  125.0 11.3 %dynamic_update_slice.6 = f32[8,256,7,64]{1,0,3,2:T(8,128)} dynamic-update-slice(f32[8,256,7,64]{1,0,3,2:T(8,128)} %get-tuple-element.315, f32[1,256,7,64]{1,0,3,2:T(1,128)} %copy.140, s32[]{:T(128)} %get-tuple-element.313, s32[]{:T(128)} %constant.69.clone.1..sunk, s32[]{:T(128)} %constant.69.clone.1..sunk, s32[]{:T(128)} %constant.69.clone.1..sunk) | dynamic-update-slice | bytes 917508 | tf_op jit(solution)/shard_map/while/body/jit(dynamic_update_index_in_dim)/dynamic_update_slice | solution.py:97
  152.1 11.3 %dynamic_update_slice.6 = f32[8,256,7,64]{1,0,3,2:T(8,128)} dynamic-update-slice(f32[8,256,7,64]{1,0,3,2:T(8,128)} %get-tuple-element.315, f32[1,256,7,64]{1,0,3,2:T(1,128)} %copy.140, s32[]{:T(128)} %get-tuple-element.313, s32[]{:T(128)} %constant.69.clone.1..sunk, s32[]{:T(128)} %constant.69.clone.1..sunk, s32[]{:T(128)} %constant.69.clone.1..sunk) | dynamic-update-slice | bytes 917508 | tf_op jit(solution)/shard_map/while/body/jit(dynamic_update_index_in_dim)/dynamic_update_slice | solution.py:97
  179.3 11.3 %dynamic_update_slice.6 = f32[8,256,7,64]{1,0,3,2:T(8,128)} dynamic-update-slice(f32[8,256,7,64]{1,0,3,2:T(8,128)} %get-tuple-element.315, f32[1,256,7,64]{1,0,3,2:T(1,128)} %copy.140, s32[]{:T(128)} %get-tuple-element.313, s32[]{:T(128)} %constant.69.clone.1..sunk, s32[]{:T(128)} %constant.69.clone.1..sunk, s32[]{:T(128)} %constant.69.clone.1..sunk) | dynamic-update-slice | bytes 917508 | tf_op jit(solution)/shard_map/while/body/jit(dynamic_update_index_in_dim)/dynamic_update_slice | solution.py:97
  206.4 11.3 %dynamic_update_slice.6 = f32[8,256,7,64]{1,0,3,2:T(8,128)} dynamic-update-slice(f32[8,256,7,64]{1,0,3,2:T(8,128)} %get-tuple-element.315, f32[1,256,7,64]{1,0,3,2:T(1,128)} %copy.140, s32[]{:T(128)} %get-tuple-element.313, s32[]{:T(128)} %constant.69.clone.1..sunk, s32[]{:T(128)} %constant.69.clone.1..sunk, s32[]{:T(128)} %constant.69.clone.1..sunk) | dynamic-update-slice | bytes 917508 | tf_op jit(solution)/shard_map/while/body/jit(dynamic_update_index_in_dim)/dynamic_update_slice | solution.py:97
  233.6 11.3 %dynamic_update_slice.6 = f32[8,256,7,64]{1,0,3,2:T(8,128)} dynamic-update-slice(f32[8,256,7,64]{1,0,3,2:T(8,128)} %get-tuple-element.315, f32[1,256,7,64]{1,0,3,2:T(1,128)} %copy.140, s32[]{:T(128)} %get-tuple-element.313, s32[]{:T(128)} %constant.69.clone.1..sunk, s32[]{:T(128)} %constant.69.clone.1..sunk, s32[]{:T(128)} %constant.69.clone.1..sunk) | dynamic-update-slice | bytes 917508 | tf_op jit(solution)/shard_map/while/body/jit(dynamic_update_index_in_dim)/dynamic_update_slice | solution.py:97
  252.5 92.2 %psum.7 = f32[2048,2]{0,1:T(2,128)S(1)} all-reduce(f32[2048,2]{0,1:T(2,128)S(1)} %broadcast_multiply_fusion.1), channel_id=1, replica_groups=mesh['dp'=16,'tensor'=16] {'tensor'}, use_global_device_ids=true, to_apply=%region_5.6 | all-reduce | flops 4096 | bytes 32768 | tf_op jit(solution)/shard_map/psum | solution.py:124
  344.8 3.9 copy.89
  348.7 11.6 %convolution_convert_fusion = bf16[2048,3584]{1,0:T(8,128)(2,1)} fusion(bf16[448,3584]{1,0:T(8,128)(2,1)S(1)} %copy-done, f32[2048,448]{0,1:T(8,128)S(1)} %bitcast.258, f32[448]{0:T(512)S(1)} %copy-done.13, f32[2048]{0:T(1024)S(1)} %add_rsqrt_fusion, bf16[1,2048,448]{1,2,0:T(8,128)(2,1)S(1)} %copy-done.4), kind=kOutput, calls=%fused_computation.84 | convolution fusion | flops 6592266240 | bytes 23406336 | tf_op jit(solution)/shard_map/dot_general | solution.py:130
  364.6 2.1 convolution_add_fusion.3
  366.7 2.7 reshape.350
  369.4 3.4 copy.134
  372.8 3.3 reshape.351
  376.3 2.3 convolution_convert_fusion.1
  380.1 6.6 %all-to-all-start = ((bf16[16,7,4096]{2,1,0:T(8,128)(2,1)}), bf16[16,7,4096]{2,1,0:T(8,128)(2,1)}, u32[]{:S(2)}, u32[]{:S(2)}) async-start(bf16[16,7,4096]{2,1,0:T(8,128)(2,1)} %copy.69), calls=%async_computation.1 | async-start | bytes 2097152 | tf_op jit(solution)/shard_map/all_to_all | solution.py:143
  386.7 17.7 %all-to-all-done = bf16[16,7,4096]{2,1,0:T(8,128)(2,1)} async-done(((bf16[16,7,4096]{2,1,0:T(8,128)(2,1)}), bf16[16,7,4096]{2,1,0:T(8,128)(2,1)}, u32[]{:S(2)}, u32[]{:S(2)}) %all-to-all-start) | async-done | bytes 917536 | tf_op jit(solution)/shard_map/all_to_all | solution.py:143
  404.5 3.2 fusion.83
  407.7 142.0 %reduce-scatter.2.cloned.1.call-done = bf16[128,3584]{1,0:T(8,128)(2,1)} async-done(((bf16[2048,3584]{1,0:T(8,128)(2,1)}), bf16[128,3584]{1,0:T(8,128)(2,1)}) %reduce-scatter.2.cloned.1.call-update) | async-done | bytes 917520 | tf_op jit(solution)/shard_map/reduce_scatter | solution.py:129
  (265 shorter events, 142.1 us)
Async XLA Ops:
  7.2 341.5 %copy-start = (bf16[448,3584]{1,0:T(8,128)(2,1)S(1)}, bf16[448,3584]{1,0:T(8,128)(2,1)}, u32[]{:S(2)}) copy-start(bf16[448,3584]{1,0:T(8,128)(2,1)} %param.21) | copy-start | bytes 9633796
  7.2 542.6 %reduce-scatter.2.cloned.1.call-start = ((), (), s32[]{:S(2)}) async-start(), calls=%async_computation.2 | async-start | bytes 15597568 | tf_op jit(solution)/shard_map/reduce_scatter | solution.py:129
  7.8 8.5 %copy-start.14 = (f32[7]{0:T(128)S(1)}, f32[7]{0:T(128)}, u32[]{:S(2)}) copy-start(f32[7]{0:T(128)} %param.18) | copy-start | bytes 88
  7.8 8.5 %copy-start.7 = (f32[1,2048,7]{1,0,2:T(1,128)S(1)}, f32[1,2048,7]{1,0,2:T(1,128)}, u32[]{:S(2)}) copy-start(f32[1,2048,7]{1,0,2:T(1,128)} %param.17) | copy-start | bytes 172036
  23.3 5.3 copy-start.8
  36.7 3.7 copy-start.15
  42.3 14.9 %copy-start.11 = (f32[8,7]{1,0:T(8,128)S(1)}, f32[8,7]{1,0:T(8,128)}, u32[]{:S(2)}) copy-start(f32[8,7]{1,0:T(8,128)} %copy-done.10) | copy-start | bytes 676 | tf_op jit(solution)/shard_map/while
  63.9 3.7 copy-start.15
  69.4 14.9 %copy-start.11 = (f32[8,7]{1,0:T(8,128)S(1)}, f32[8,7]{1,0:T(8,128)}, u32[]{:S(2)}) copy-start(f32[8,7]{1,0:T(8,128)} %copy-done.10) | copy-start | bytes 676 | tf_op jit(solution)/shard_map/while
  91.0 3.7 copy-start.15
  96.6 14.9 %copy-start.11 = (f32[8,7]{1,0:T(8,128)S(1)}, f32[8,7]{1,0:T(8,128)}, u32[]{:S(2)}) copy-start(f32[8,7]{1,0:T(8,128)} %copy-done.10) | copy-start | bytes 676 | tf_op jit(solution)/shard_map/while
  118.2 3.7 copy-start.15
  123.7 14.9 %copy-start.11 = (f32[8,7]{1,0:T(8,128)S(1)}, f32[8,7]{1,0:T(8,128)}, u32[]{:S(2)}) copy-start(f32[8,7]{1,0:T(8,128)} %copy-done.10) | copy-start | bytes 676 | tf_op jit(solution)/shard_map/while
  145.3 3.7 copy-start.15
  150.9 14.9 %copy-start.11 = (f32[8,7]{1,0:T(8,128)S(1)}, f32[8,7]{1,0:T(8,128)}, u32[]{:S(2)}) copy-start(f32[8,7]{1,0:T(8,128)} %copy-done.10) | copy-start | bytes 676 | tf_op jit(solution)/shard_map/while
  172.5 3.7 copy-start.15
  178.0 14.9 %copy-start.11 = (f32[8,7]{1,0:T(8,128)S(1)}, f32[8,7]{1,0:T(8,128)}, u32[]{:S(2)}) copy-start(f32[8,7]{1,0:T(8,128)} %copy-done.10) | copy-start | bytes 676 | tf_op jit(solution)/shard_map/while
  199.6 3.7 copy-start.15
  205.2 14.9 %copy-start.11 = (f32[8,7]{1,0:T(8,128)S(1)}, f32[8,7]{1,0:T(8,128)}, u32[]{:S(2)}) copy-start(f32[8,7]{1,0:T(8,128)} %copy-done.10) | copy-start | bytes 676 | tf_op jit(solution)/shard_map/while
  226.8 3.7 copy-start.15
  232.3 14.9 %copy-start.11 = (f32[8,7]{1,0:T(8,128)S(1)}, f32[8,7]{1,0:T(8,128)}, u32[]{:S(2)}) copy-start(f32[8,7]{1,0:T(8,128)} %copy-done.10) | copy-start | bytes 676 | tf_op jit(solution)/shard_map/while
  344.8 3.9 copy-start.4
  344.8 3.9 copy-start.13
  380.1 24.4 %all-to-all-start = ((bf16[16,7,4096]{2,1,0:T(8,128)(2,1)}), bf16[16,7,4096]{2,1,0:T(8,128)(2,1)}, u32[]{:S(2)}, u32[]{:S(2)}) async-start(bf16[16,7,4096]{2,1,0:T(8,128)(2,1)} %copy.69), calls=%async_computation.1 | async-start | bytes 2097152 | tf_op jit(solution)/shard_map/all_to_all | solution.py:143
  (15 other events, 40.4 us)
Sparse Core Ops, SparseCore 0:
  360.5 189.1 reduce-scatter.1
where the time goes:
time: 562 us; the launch traced here: 557 us
  waiting for transfers between devices  160 us (28%)
  local copies, waits for them, and re-layouts  158 us (28%)
  blocking collectives  92.2 us (16%)
  matrix products  90.4 us (16%)
  other arithmetic  23.5 us (4%)
  between operations  14.3 us (3%)
  loops' own time  11.8 us (2%)
  starting transfers between devices  6.61 us (1%)
    reduce_scatter x1, waiting for transfers between devices, local(): lax.psum_scatter(jnp.dot(rounded, out_weight, preferred_element_type=jnp....  142 us
    dynamic_update_slice x16, local copies, waits for them, and re-layouts, local(): lax.scan(advance, jnp.zeros((dev_heads, HEAD, STATE), jnp.float32), block...  100 us
    psum x1, blocking collectives, local(): group_stat = lax.psum(sum_sq[:, None] * group_hot[None, :], 'tensor')  92.2 us
    dot_general x25, matrix products, split_einsum(): jnp.einsum(form, lower, narrow, preferred_element_type=jnp.float32)  33.6 us
    dot_general x25, matrix products, split_einsum(): first = jnp.einsum(form, upper, narrow, preferred_element_type=jnp.float32)  30.6 us
    all_to_all x1, waiting for transfers between devices, local(): lax.all_to_all(outbound.astype(jnp.bfloat16), 'dp', split_axis=0, concat_...  17.7 us
    unnamed x39, local copies, waits for them, and re-layouts  17.2 us
    dynamic_slice x24, local copies, waits for them, and re-layouts, local(): lax.scan(advance, jnp.zeros((dev_heads, HEAD, STATE), jnp.float32), block...  16.8 us
  transfers between devices with their start and end apart: 2, of which 2 were waited for; matrix products, arithmetic and copies ran while one was open for 4% of the time, Pallas kernels for 0%

commit v1 on v0

--- a/solution.py
+++ b/solution.py
@@ -11,6 +11,12 @@
 BLOCK = 256
 INNER = 7168
 HIGHEST = lax.Precision.HIGHEST
+
+
+def summed_here(shard, axis):
+    blocks = lax.all_gather(shard, axis, axis=0, tiled=False)
+    total = blocks.sum(axis=0)
+    return total
 
 
 def split_pair(values):
@@ -121,7 +127,7 @@
     gated = mixer_y * jax.nn.silu(gate_z[0].astype(jnp.float32))
     sum_sq = jnp.sum(gated * gated, axis=1)
     group_hot = (jnp.arange(NGROUPS) == group_idx).astype(jnp.float32)
-    group_stat = lax.psum(sum_sq[:, None] * group_hot[None, :], "tensor")
+    group_stat = summed_here(sum_sq[:, None] * group_hot[None, :], "tensor")
     mean_sq = jnp.sum(group_stat * group_hot[None, :], axis=1) / (INNER // NGROUPS)
     rounded = (gated * lax.rsqrt(mean_sq + 1e-05)[:, None] * norm_gain[None, :]).astype(
         jnp.bfloat16

time: 562 us -> 505 us (0.90)
  blocking collectives: 92.2 us -> 35 us
    psum x1 -> x0, blocking collectives: 92.2 us -> none  [local(): group_stat = lax.psum(sum_sq[:, None] * group_hot[None, :], 'tensor')]
    reduce_scatter x1, waiting for transfers between devices: 142 us -> 72.5 us  [local(): lax.psum_scatter(jnp.dot(rounded, out_weight, preferred_element_type=jnp....]
    all_to_all x1, waiting for transfers between devices: 17.7 us -> 85.4 us  [local(): lax.all_to_all(outbound.astype(jnp.bfloat16), 'dp', split_axis=0, concat_...]
    all_gather x0 -> x1, blocking collectives: none -> 35 us  [summed_here(): blocks = lax.all_gather(shard, axis, axis=0, tiled=False)]
where the time goes in v1:
time: 505 us; the launch traced here: 499 us
  local copies, waits for them, and re-layouts  158 us (31%)
  waiting for transfers between devices  158 us (31%)
  matrix products  89.8 us (18%)
  blocking collectives  35 us (7%)
  other arithmetic  25.5 us (5%)
  between operations  14.3 us (3%)
  loops' own time  11.8 us (2%)
  starting transfers between devices  6.69 us (1%)
    dynamic_update_slice x16, local copies, waits for them, and re-layouts, local(): lax.scan(advance, jnp.zeros((dev_heads, HEAD, STATE), jnp.float32), block...  100 us
    all_to_all x1, waiting for transfers between devices, local(): lax.all_to_all(outbound.astype(jnp.bfloat16), 'dp', split_axis=0, concat_...  85.4 us
    reduce_scatter x1, waiting for transfers between devices, local(): lax.psum_scatter(jnp.dot(rounded, out_weight, preferred_element_type=jnp....  72.5 us
    all_gather x1, blocking collectives, summed_here(): blocks = lax.all_gather(shard, axis, axis=0, tiled=False)  35 us
    dot_general x25, matrix products, split_einsum(): jnp.einsum(form, lower, narrow, preferred_element_type=jnp.float32)  33.6 us
    dot_general x25, matrix products, split_einsum(): first = jnp.einsum(form, upper, narrow, preferred_element_type=jnp.float32)  30.6 us
    unnamed x39, local copies, waits for them, and re-layouts  17.2 us
    dynamic_slice x24, local copies, waits for them, and re-layouts, local(): lax.scan(advance, jnp.zeros((dev_heads, HEAD, STATE), jnp.float32), block...  16.8 us
  transfers between devices with their start and end apart: 2, of which 2 were waited for; matrix products, arithmetic and copies ran while one was open for 4% of the time, Pallas kernels for 0%

profile of v1, /device:TPU:32, one launch (start us, length us, event | category | flops | bytes accessed | tf_op | source)
XLA Modules:
  0.0 499.0 jit_solution(18085652721575162115)
XLA Ops:
  7.8 2.8 constant_dynamic-slice_fusion.3
  16.4 2.0 reduce-window.6
  21.2 2.1 copy.102
  30.0 217.2 %while.13 = (s32[]{:T(128)}, f32[7,64,64]{2,1,0:T(8,128)S(1)}, f32[8,256,7,64]{1,0,3,2:T(8,128)}, f32[8,256,7]{1,2,0:T(8,128)S(1)}, f32[8,7]{1,0:T(8,128)S(1)}, ...) while((s32[]{:T(128)}, f32[7,64,64]{2,1,0:T(8,128)S(1)}, ...), condition=%wide.region_3.4_spmd.clone, body=%wide.region_2.3_spmd.clone.sunk | while | flops 192841488 | bytes 8220087 | solution.py:103
  43.5 11.3 %dynamic_update_slice.6 = f32[8,256,7,64]{1,0,3,2:T(8,128)} dynamic-update-slice(f32[8,256,7,64]{1,0,3,2:T(8,128)} %get-tuple-element.327, f32[1,256,7,64]{1,0,3,2:T(1,128)} %copy.155, s32[]{:T(128)} %get-tuple-element.325, s32[]{:T(128)} %constant.69.clone.1..sunk, s32[]{:T(128)} %constant.69.clone.1..sunk, s32[]{:T(128)} %constant.69.clone.1..sunk) | dynamic-update-slice | bytes 917508 | tf_op jit(solution)/shard_map/while/body/jit(dynamic_update_index_in_dim)/dynamic_update_slice | solution.py:103
  70.7 11.3 %dynamic_update_slice.6 = f32[8,256,7,64]{1,0,3,2:T(8,128)} dynamic-update-slice(f32[8,256,7,64]{1,0,3,2:T(8,128)} %get-tuple-element.327, f32[1,256,7,64]{1,0,3,2:T(1,128)} %copy.155, s32[]{:T(128)} %get-tuple-element.325, s32[]{:T(128)} %constant.69.clone.1..sunk, s32[]{:T(128)} %constant.69.clone.1..sunk, s32[]{:T(128)} %constant.69.clone.1..sunk) | dynamic-update-slice | bytes 917508 | tf_op jit(solution)/shard_map/while/body/jit(dynamic_update_index_in_dim)/dynamic_update_slice | solution.py:103
  97.8 11.3 %dynamic_update_slice.6 = f32[8,256,7,64]{1,0,3,2:T(8,128)} dynamic-update-slice(f32[8,256,7,64]{1,0,3,2:T(8,128)} %get-tuple-element.327, f32[1,256,7,64]{1,0,3,2:T(1,128)} %copy.155, s32[]{:T(128)} %get-tuple-element.325, s32[]{:T(128)} %constant.69.clone.1..sunk, s32[]{:T(128)} %constant.69.clone.1..sunk, s32[]{:T(128)} %constant.69.clone.1..sunk) | dynamic-update-slice | bytes 917508 | tf_op jit(solution)/shard_map/while/body/jit(dynamic_update_index_in_dim)/dynamic_update_slice | solution.py:103
  125.0 11.3 %dynamic_update_slice.6 = f32[8,256,7,64]{1,0,3,2:T(8,128)} dynamic-update-slice(f32[8,256,7,64]{1,0,3,2:T(8,128)} %get-tuple-element.327, f32[1,256,7,64]{1,0,3,2:T(1,128)} %copy.155, s32[]{:T(128)} %get-tuple-element.325, s32[]{:T(128)} %constant.69.clone.1..sunk, s32[]{:T(128)} %constant.69.clone.1..sunk, s32[]{:T(128)} %constant.69.clone.1..sunk) | dynamic-update-slice | bytes 917508 | tf_op jit(solution)/shard_map/while/body/jit(dynamic_update_index_in_dim)/dynamic_update_slice | solution.py:103
  152.1 11.3 %dynamic_update_slice.6 = f32[8,256,7,64]{1,0,3,2:T(8,128)} dynamic-update-slice(f32[8,256,7,64]{1,0,3,2:T(8,128)} %get-tuple-element.327, f32[1,256,7,64]{1,0,3,2:T(1,128)} %copy.155, s32[]{:T(128)} %get-tuple-element.325, s32[]{:T(128)} %constant.69.clone.1..sunk, s32[]{:T(128)} %constant.69.clone.1..sunk, s32[]{:T(128)} %constant.69.clone.1..sunk) | dynamic-update-slice | bytes 917508 | tf_op jit(solution)/shard_map/while/body/jit(dynamic_update_index_in_dim)/dynamic_update_slice | solution.py:103
  179.3 11.3 %dynamic_update_slice.6 = f32[8,256,7,64]{1,0,3,2:T(8,128)} dynamic-update-slice(f32[8,256,7,64]{1,0,3,2:T(8,128)} %get-tuple-element.327, f32[1,256,7,64]{1,0,3,2:T(1,128)} %copy.155, s32[]{:T(128)} %get-tuple-element.325, s32[]{:T(128)} %constant.69.clone.1..sunk, s32[]{:T(128)} %constant.69.clone.1..sunk, s32[]{:T(128)} %constant.69.clone.1..sunk) | dynamic-update-slice | bytes 917508 | tf_op jit(solution)/shard_map/while/body/jit(dynamic_update_index_in_dim)/dynamic_update_slice | solution.py:103
  206.4 11.3 %dynamic_update_slice.6 = f32[8,256,7,64]{1,0,3,2:T(8,128)} dynamic-update-slice(f32[8,256,7,64]{1,0,3,2:T(8,128)} %get-tuple-element.327, f32[1,256,7,64]{1,0,3,2:T(1,128)} %copy.155, s32[]{:T(128)} %get-tuple-element.325, s32[]{:T(128)} %constant.69.clone.1..sunk, s32[]{:T(128)} %constant.69.clone.1..sunk, s32[]{:T(128)} %constant.69.clone.1..sunk) | dynamic-update-slice | bytes 917508 | tf_op jit(solution)/shard_map/while/body/jit(dynamic_update_index_in_dim)/dynamic_update_slice | solution.py:103
  233.6 11.3 %dynamic_update_slice.6 = f32[8,256,7,64]{1,0,3,2:T(8,128)} dynamic-update-slice(f32[8,256,7,64]{1,0,3,2:T(8,128)} %get-tuple-element.327, f32[1,256,7,64]{1,0,3,2:T(1,128)} %copy.155, s32[]{:T(128)} %get-tuple-element.325, s32[]{:T(128)} %constant.69.clone.1..sunk, s32[]{:T(128)} %constant.69.clone.1..sunk, s32[]{:T(128)} %constant.69.clone.1..sunk) | dynamic-update-slice | bytes 917508 | tf_op jit(solution)/shard_map/while/body/jit(dynamic_update_index_in_dim)/dynamic_update_slice | solution.py:103
  252.5 35.0 %all_gather.4 = f32[16,2048,2]{1,2,0:T(2,128)} all-gather(f32[1,2048,2]{1,2,0:T(2,128)S(1)} %broadcast_multiply_fusion.1), channel_id=1, replica_groups=mesh['dp'=16,'tensor'=16] {'tensor'}, dimensions={0}, use_global_device_ids=true | all-gather | bytes 278528 | tf_op jit(solution)/shard_map/all_gather | solution.py:17
  288.7 3.9 copy.104
  292.6 11.8 %convolution_convert_fusion = bf16[2048,3584]{1,0:T(8,128)(2,1)} fusion(bf16[448,3584]{1,0:T(8,128)(2,1)S(1)} %copy-done, f32[2048,448]{0,1:T(8,128)S(1)} %bitcast.258, f32[448]{0:T(512)S(1)} %copy-done.13, f32[2048]{0:T(1024)S(1)} %add_rsqrt_fusion, bf16[1,2048,448]{1,2,0:T(8,128)(2,1)S(1)} %copy-done.3), kind=kOutput, calls=%fused_computation.84 | convolution fusion | flops 6592266240 | bytes 23406336 | tf_op jit(solution)/shard_map/dot_general | solution.py:136
  308.8 2.1 convolution_add_fusion.3
  310.9 2.7 reshape.402
  313.5 3.5 copy.149
  317.0 3.3 reshape.403
  320.5 2.3 convolution_convert_fusion.1
  324.3 6.7 %all-to-all-start = ((bf16[16,7,4096]{2,1,0:T(8,128)(2,1)}), bf16[16,7,4096]{2,1,0:T(8,128)(2,1)}, u32[]{:S(2)}, u32[]{:S(2)}) async-start(bf16[16,7,4096]{2,1,0:T(8,128)(2,1)} %copy.83), calls=%async_computation.1 | async-start | bytes 2097152 | tf_op jit(solution)/shard_map/all_to_all | solution.py:149
  331.0 85.4 %all-to-all-done = bf16[16,7,4096]{2,1,0:T(8,128)(2,1)} async-done(((bf16[16,7,4096]{2,1,0:T(8,128)(2,1)}), bf16[16,7,4096]{2,1,0:T(8,128)(2,1)}, u32[]{:S(2)}, u32[]{:S(2)}) %all-to-all-start) | async-done | bytes 917536 | tf_op jit(solution)/shard_map/all_to_all | solution.py:149
  416.4 3.2 fusion.83
  419.7 72.5 %reduce-scatter.2.cloned.1.call-done = bf16[128,3584]{1,0:T(8,128)(2,1)} async-done(((bf16[2048,3584]{1,0:T(8,128)(2,1)}), bf16[128,3584]{1,0:T(8,128)(2,1)}) %reduce-scatter.2.cloned.1.call-update) | async-done | bytes 917520 | tf_op jit(solution)/shard_map/reduce_scatter | solution.py:135
  (266 shorter events, 143.3 us)
Async XLA Ops:
  7.2 285.4 %copy-start = (bf16[448,3584]{1,0:T(8,128)(2,1)S(1)}, bf16[448,3584]{1,0:T(8,128)(2,1)}, u32[]{:S(2)}) copy-start(bf16[448,3584]{1,0:T(8,128)(2,1)} %param.21) | copy-start | bytes 9633796
  7.2 485.0 %reduce-scatter.2.cloned.1.call-start = ((), (), s32[]{:S(2)}) async-start(), calls=%async_computation.2 | async-start | bytes 15597568 | tf_op jit(solution)/shard_map/reduce_scatter | solution.py:135
  7.8 8.5 %copy-start.14 = (f32[7]{0:T(128)S(1)}, f32[7]{0:T(128)}, u32[]{:S(2)}) copy-start(f32[7]{0:T(128)} %param.18) | copy-start | bytes 88
  7.8 8.5 %copy-start.6 = (f32[1,2048,7]{1,0,2:T(1,128)S(1)}, f32[1,2048,7]{1,0,2:T(1,128)}, u32[]{:S(2)}) copy-start(f32[1,2048,7]{1,0,2:T(1,128)} %param.17) | copy-start | bytes 172036
  23.3 5.3 %copy-start.8 = (s32[1,2048]{1,0:T(1,128)S(1)}, s32[1,2048]{1,0:T(1,128)}, u32[]{:S(2)}) copy-start(s32[1,2048]{1,0:T(1,128)} %param.22) | copy-start | bytes 24580
  36.7 3.7 copy-start.15
  42.3 14.9 %copy-start.11 = (f32[8,7]{1,0:T(8,128)S(1)}, f32[8,7]{1,0:T(8,128)}, u32[]{:S(2)}) copy-start(f32[8,7]{1,0:T(8,128)} %copy-done.10) | copy-start | bytes 676 | tf_op jit(solution)/shard_map/while
  63.9 3.7 copy-start.15
  69.4 14.9 %copy-start.11 = (f32[8,7]{1,0:T(8,128)S(1)}, f32[8,7]{1,0:T(8,128)}, u32[]{:S(2)}) copy-start(f32[8,7]{1,0:T(8,128)} %copy-done.10) | copy-start | bytes 676 | tf_op jit(solution)/shard_map/while
  91.0 3.7 copy-start.15
  96.6 14.9 %copy-start.11 = (f32[8,7]{1,0:T(8,128)S(1)}, f32[8,7]{1,0:T(8,128)}, u32[]{:S(2)}) copy-start(f32[8,7]{1,0:T(8,128)} %copy-done.10) | copy-start | bytes 676 | tf_op jit(solution)/shard_map/while
  118.2 3.7 copy-start.15
  123.7 14.9 %copy-start.11 = (f32[8,7]{1,0:T(8,128)S(1)}, f32[8,7]{1,0:T(8,128)}, u32[]{:S(2)}) copy-start(f32[8,7]{1,0:T(8,128)} %copy-done.10) | copy-start | bytes 676 | tf_op jit(solution)/shard_map/while
  145.3 3.7 copy-start.15
  150.9 14.9 %copy-start.11 = (f32[8,7]{1,0:T(8,128)S(1)}, f32[8,7]{1,0:T(8,128)}, u32[]{:S(2)}) copy-start(f32[8,7]{1,0:T(8,128)} %copy-done.10) | copy-start | bytes 676 | tf_op jit(solution)/shard_map/while
  172.5 3.7 copy-start.15
  178.0 14.9 %copy-start.11 = (f32[8,7]{1,0:T(8,128)S(1)}, f32[8,7]{1,0:T(8,128)}, u32[]{:S(2)}) copy-start(f32[8,7]{1,0:T(8,128)} %copy-done.10) | copy-start | bytes 676 | tf_op jit(solution)/shard_map/while
  199.6 3.7 copy-start.15
  205.2 14.9 %copy-start.11 = (f32[8,7]{1,0:T(8,128)S(1)}, f32[8,7]{1,0:T(8,128)}, u32[]{:S(2)}) copy-start(f32[8,7]{1,0:T(8,128)} %copy-done.10) | copy-start | bytes 676 | tf_op jit(solution)/shard_map/while
  226.8 3.7 copy-start.15
  232.3 14.9 %copy-start.11 = (f32[8,7]{1,0:T(8,128)S(1)}, f32[8,7]{1,0:T(8,128)}, u32[]{:S(2)}) copy-start(f32[8,7]{1,0:T(8,128)} %copy-done.10) | copy-start | bytes 676 | tf_op jit(solution)/shard_map/while
  288.7 3.9 copy-start.3
  288.7 3.9 copy-start.13
  324.3 92.2 %all-to-all-start = ((bf16[16,7,4096]{2,1,0:T(8,128)(2,1)}), bf16[16,7,4096]{2,1,0:T(8,128)(2,1)}, u32[]{:S(2)}, u32[]{:S(2)}) async-start(bf16[16,7,4096]{2,1,0:T(8,128)(2,1)} %copy.83), calls=%async_computation.1 | async-start | bytes 2097152 | tf_op jit(solution)/shard_map/all_to_all | solution.py:149
  (15 other events, 39.4 us)
Sparse Core Ops, SparseCore 0:
  304.6 187.5 reduce-scatter.1
